TPU v7x, 128 devices: a whole 4x4x4 slice. The times are simulated.
128 devices in a mesh: half: 2 (over core), row: 8 (over z_hi, x), col: 8 (over y, z_lo).
Axes of the slice: x: 4, y: 4, z: 4 (z_hi: 2, z_lo: 2; z = z_hi * 2 + z_lo), core: 2. Of those that a mesh axis runs over, the one named last changes fastest.
Arguments:
- child_diag: float32 [2, 512, 512], P('half'), as said below
- child_panel: float32 [2, 16, 8, 128, 512], P('half', None, 'row'), may hold values from -18 to 18
- child_window: float32 [2, 16, 8, 128, 8, 8, 128], P('half', None, 'row', None, None, 'col'), may hold values from -6 to 6
- parent_diag: float32 [512, 512], replicated
- parent_lead_panel: float32 [24, 8, 2, 8, 8, 512], P(None, 'row', 'half', 'col'), may hold values from -24 to 24
- index_maps: int32 [2, 128], replicated, may hold values from 0 to 191, as said below
Outputs:
- parent_front: float32 [24, 8, 128, 4, 2, 8, 128], P(None, 'row', None, None, 'half', 'col')
- parent_factor: float32 [24, 8, 2, 8, 8, 512], P(None, 'row', 'half', 'col')
- parent_pivot: float32 [512, 512], replicated
Inputs may be any that keep to these rules, and one draw needn't show every extreme that they name: child_diag and parent_diag are symmetric and positive definite. For each child k and each group a, the entries index_maps[k, a * 16 + u] with 0 <= u < 16 equal q * 16 + ((u + s) mod 16) for a group target q and a turn s fixed within the group; groups a < 4 have q = a, later groups have distinct q that rise with a; over the 8 groups of a child the turns s, taken modulo 8, are all different; for each child some group a < 4 has a turn divisible by 8, and another group a < 4 has a turn that leaves 1 modulo 8.
All inputs are finite; a program needn't handle non-finite values.
Results may differ from a plain program's by a relative error of at most 0.0001.
Values sent between devices are 32-bit elements; how exact they have to be, the bound alone decides.
No kernel may reach another device: no remote copies, remote signals or barrier semaphores. Data moves between devices by JAX's collectives and lax.ppermute only.
A program may use at most 192 MiB of HBM per device.

v0:
```python
import jax
import jax.numpy as jnp
from jax import lax
from jax.sharding import PartitionSpec as P

BLOCK_EXTENT = 128
PB = 4
SB = 128
RB = 192
WB = 64


def from_root(shard, axis, root):
    mine = lax.axis_index(axis) == root
    return lax.psum(jnp.where(mine, shard, jnp.zeros_like(shard)), axis)


def pick_ranked(owners, values, wanted, slot_count, missing):
    matches = owners[..., None, :] == wanted[:, None]
    ranking = jnp.cumsum(matches.astype(jnp.int32), axis=-1) - 1
    slot_ids = jnp.arange(slot_count, dtype=jnp.int32)
    chosen = matches[..., None, :] & (ranking[..., None, :] == slot_ids[:, None])
    present = jnp.any(chosen, axis=-1)
    picked = jnp.sum(jnp.where(chosen, values[..., None, None, :], 0), axis=-1)
    return jnp.where(present, picked, missing)


def _dot_t(x, y):
    return lax.dot_general(x, y, (((1,), (1,)), ((), ())), precision=lax.Precision.HIGHEST)


def _dot(x, y):
    return jnp.dot(x, y, precision=lax.Precision.HIGHEST)


def factor_and_inverse(spd, leaf):
    order = spd.shape[0]
    blocks = order // leaf
    work = spd
    columns = []
    inverses = []
    eye = jnp.eye(leaf, dtype=spd.dtype)
    for k in range(blocks):
        low = jnp.linalg.cholesky(work[:leaf, :leaf])
        inv = lax.linalg.triangular_solve(low, eye, left_side=True, lower=True)
        inverses.append(inv)
        if k < blocks - 1:
            below = _dot_t(work[leaf:, :leaf], inv)
            work = work[leaf:, leaf:] - _dot_t(below, below)
            columns.append(jnp.concatenate([low, below], axis=0))
        else:
            columns.append(low)
    lower = jnp.concatenate(
        [jnp.pad(c, ((order - c.shape[0], 0), (0, 0))) for c in columns], axis=1
    )
    size = leaf
    while len(inverses) > 1:
        merged = []
        for t in range(0, len(inverses), 2):
            start = t * size
            first, second = (inverses[t], inverses[t + 1])
            coupling = lower[start + size : start + 2 * size, start : start + size]
            corner = -_dot(second, _dot(coupling, first))
            top = jnp.concatenate([first, jnp.zeros_like(first)], axis=1)
            bottom = jnp.concatenate([corner, second], axis=1)
            merged.append(jnp.concatenate([top, bottom], axis=0))
        inverses = merged
        size *= 2
    return (lower, inverses[0])


def per_device(child_diag, child_panel, child_window, parent_diag, parent_lead_panel, index_maps):
    highest = lax.Precision.HIGHEST
    row_size = lax.axis_size("row")
    col_size = lax.axis_size("col")
    half_id = lax.axis_index("half")
    row_id = lax.axis_index("row")
    col_id = lax.axis_index("col")
    panel_width = PB * BLOCK_EXTENT
    group_size = 2 * row_size
    row_local = SB // row_size
    col_local = WB // row_size
    parent_row_blocks = RB // row_size
    parent_cols = WB // group_size
    per_row = 2 * (SB // group_size) // row_size
    per_col = (WB // group_size + row_size - 1) // row_size
    transpose_perm = [
        (i * col_size + j, j * row_size + i)
        for i in range(row_size)
        for j in range(col_size)
        if i != j
    ]
    on_diagonal = row_id == col_id
    child_lead = child_panel[0, :col_local, 0]
    child_col_rows = jnp.where(
        on_diagonal, child_lead, lax.ppermute(child_lead, ("row", "col"), transpose_perm)
    )
    sub_rows = parent_lead_panel.shape[4]
    own_rows = parent_lead_panel.reshape(-1, panel_width)
    gathered = lax.all_gather(
        parent_lead_panel.reshape(parent_row_blocks, sub_rows, panel_width),
        ("half", "col"),
        axis=1,
        tiled=True,
    )
    leading_parent = parent_lead_panel.reshape(parent_row_blocks, sub_rows, panel_width)[
        : 2 * parent_cols
    ]
    transposed = jnp.where(
        on_diagonal, leading_parent, lax.ppermute(leading_parent, ("row", "col"), transpose_perm)
    )
    column_blocks = lax.all_gather(transposed, ("half", "row"), axis=1, tiled=True)
    parent_col_rows = lax.dynamic_index_in_dim(
        column_blocks.reshape(parent_cols, 2, BLOCK_EXTENT, panel_width),
        half_id,
        axis=1,
        keepdims=False,
    )
    child_low, child_inv = factor_and_inverse(child_diag[0], BLOCK_EXTENT)
    child_rows = child_panel.reshape(-1, panel_width)
    dims = (((1,), (1,)), ((), ()))
    high = lax.Precision.HIGH
    child_factor = lax.dot_general(child_rows, child_inv, dims, precision=high)
    child_columns = lax.dot_general(
        child_col_rows.reshape(-1, panel_width), child_inv, dims, precision=high
    )
    schur_part = child_window.reshape(
        row_local * BLOCK_EXTENT, col_local * BLOCK_EXTENT
    ) - lax.dot_general(child_factor, child_columns, dims, precision=high)
    child_map = lax.dynamic_index_in_dim(index_maps, half_id, axis=0, keepdims=False)
    my_rows = lax.dynamic_index_in_dim(
        child_map.reshape(row_local, row_size), row_id, axis=1, keepdims=False
    )
    my_cols = lax.dynamic_index_in_dim(
        child_map[:WB].reshape(col_local, row_size), col_id, axis=1, keepdims=False
    )
    local_rows = jnp.arange(row_local, dtype=jnp.int32)
    local_cols = jnp.arange(col_local, dtype=jnp.int32)
    send_rows = pick_ranked(
        my_rows % row_size, local_rows, jnp.arange(row_size, dtype=jnp.int32), per_row, row_local
    )
    send_cols = pick_ranked(
        my_cols % group_size,
        local_cols,
        jnp.arange(group_size, dtype=jnp.int32),
        per_col,
        col_local,
    )
    all_rows = index_maps.reshape(2, row_local, row_size).transpose(0, 2, 1)
    row_target = pick_ranked(
        all_rows % row_size, all_rows // row_size, row_id[None], per_row, parent_row_blocks
    )[:, :, 0, :]
    all_cols = index_maps[:, :WB].reshape(2, col_local, row_size).transpose(0, 2, 1)
    col_target = pick_ranked(
        all_cols % group_size,
        all_cols // group_size,
        (half_id * row_size + col_id)[None],
        per_col,
        parent_cols,
    )[:, :, 0, :]
    schur_blocks = schur_part.reshape(row_local, BLOCK_EXTENT, col_local, BLOCK_EXTENT)
    send_row_index = jnp.minimum(send_rows, row_local - 1)[None, :, None, :, None]
    send_col_index = jnp.minimum(send_cols, col_local - 1).reshape(2, row_size, per_col)[
        :, None, :, None, :
    ]
    outgoing = schur_blocks[send_row_index, :, send_col_index, :]
    outgoing, gathered, parent_col_rows, parent_diag = lax.optimization_barrier(
        (outgoing, gathered, parent_col_rows, parent_diag)
    )
    pivot_lower_factor, parent_inv = factor_and_inverse(parent_diag, BLOCK_EXTENT)
    solved = lax.dot_general(own_rows, parent_inv, dims, precision=highest)
    parent_factor = solved.reshape(parent_lead_panel.shape)
    row_factor = lax.dot_general(
        gathered.reshape(-1, panel_width), parent_inv, dims, precision=highest
    )
    column_factor = lax.dot_general(
        parent_col_rows.reshape(-1, panel_width), parent_inv, dims, precision=highest
    )
    update = lax.dot_general(row_factor, column_factor, dims, precision=highest)
    arrived = lax.all_to_all(
        outgoing.reshape(-1, per_row * per_col, BLOCK_EXTENT, BLOCK_EXTENT),
        ("half", "row", "col"),
        split_axis=0,
        concat_axis=0,
        tiled=True,
    )
    slot_shape = (2, row_size, row_size, per_row, per_col)
    slot_rows = jnp.broadcast_to(row_target[:, :, None, :, None], slot_shape).reshape(2, -1)
    slot_cols = jnp.broadcast_to(col_target[:, None, :, None, :], slot_shape).reshape(2, -1)
    slots = slot_rows.shape[1]
    match = (
        slot_rows[:, None, None, :]
        == jnp.arange(parent_row_blocks, dtype=jnp.int32)[None, :, None, None]
    ) & (
        slot_cols[:, None, None, :] == jnp.arange(parent_cols, dtype=jnp.int32)[None, None, :, None]
    )
    slot_of = jnp.sum(jnp.where(match, jnp.arange(slots, dtype=jnp.int32), 0), axis=-1)
    present = jnp.any(match, axis=-1)
    flat_arrived = arrived.reshape(2 * slots, BLOCK_EXTENT, BLOCK_EXTENT)
    block_shape = (parent_row_blocks, parent_cols, BLOCK_EXTENT, BLOCK_EXTENT)
    first = jnp.take(flat_arrived, slot_of[0].reshape(-1), axis=0, mode="clip")
    second = jnp.take(flat_arrived, slot_of[1].reshape(-1) + slots, axis=0, mode="clip")
    assembled = jnp.where(
        present[0, :, :, None, None], first.reshape(block_shape), 0.0
    ) + jnp.where(present[1, :, :, None, None], second.reshape(block_shape), 0.0)
    updated = assembled.transpose(0, 2, 1, 3) - update.reshape(
        parent_row_blocks, BLOCK_EXTENT, parent_cols, BLOCK_EXTENT
    )
    return (
        updated.reshape(parent_row_blocks, 1, BLOCK_EXTENT, parent_cols, 1, 1, BLOCK_EXTENT),
        parent_factor,
        pivot_lower_factor,
    )


def solution(mesh):
    in_specs = (
        P("half", None, None),
        P("half", None, "row", None, None),
        P("half", None, "row", None, None, "col", None),
        P(),
        P(None, "row", "half", "col", None, None),
        P(),
    )
    out_specs = (
        P(None, "row", None, None, "half", "col", None),
        P(None, "row", "half", "col", None, None),
        P(),
    )
    return jax.shard_map(
        per_device, mesh=mesh, in_specs=in_specs, out_specs=out_specs, check_vma=False
    )
```

profile of v0, /device:TPU:10, one launch (start us, length us, event | category | flops | bytes accessed | tf_op | source)
XLA Modules:
  0.0 529.1 jit_solution(2536918463805677017)
XLA Ops:
  12.9 7.8 %collective-permute-done.1 = f32[8,8,512]{2,1,0:T(8,128)S(1)} collective-permute-done((f32[8,8,512]{2,1,0:T(8,128)S(1)}, f32[8,8,512]{2,1,0:T(8,128)S(1)}, u32[]{:S(2)}, u32[]{:S(2)}) %collective-permute-start.1) | collective-permute-done | bytes 131104 | tf_op jit(solution)/shard_map/ppermute | solution.py:110
  26.2 4.7 collective-permute-start
  35.1 11.7 %cholesky.134 = f32[128,128]{1,0:T(8,128)S(1)} custom-call(f32[128,128]{1,0:T(8,128)S(1)} %fusion.69), custom_call_target="Cholesky" | custom-call | tf_op jit(solution)/shard_map/jit(cholesky)/cholesky | solution.py:44
  48.1 9.8 %custom-call.14 = f32[1,128,128]{1,2,0:T(8,128)S(1)} custom-call(f32[1,128,128]{2,1,0:T(8,128)S(1)} %get-tuple-element.45), custom_call_target="InvertDiagBlocksLowerTriangular" | custom-call | tf_op jit(solution)/shard_map/triangular_solve/custom-call.0 | solution.py:45
  59.5 11.7 %cholesky.145 = f32[128,128]{1,0:T(8,128)S(1)} custom-call(f32[128,128]{1,0:T(8,128)S(1)} %fusion.67), custom_call_target="Cholesky" | custom-call | tf_op jit(solution)/shard_map/jit(cholesky)/cholesky | solution.py:44
  72.5 9.9 %custom-call.15 = f32[1,128,128]{1,2,0:T(8,128)S(1)} custom-call(f32[1,128,128]{2,1,0:T(8,128)S(1)} %get-tuple-element.43), custom_call_target="InvertDiagBlocksLowerTriangular" | custom-call | tf_op jit(solution)/shard_map/triangular_solve/custom-call.0 | solution.py:45
  83.9 11.7 %cholesky.156 = f32[128,128]{1,0:T(8,128)S(1)} custom-call(f32[128,128]{1,0:T(8,128)S(1)} %fusion.65), custom_call_target="Cholesky" | custom-call | tf_op jit(solution)/shard_map/jit(cholesky)/cholesky | solution.py:44
  96.9 9.8 %custom-call.16 = f32[1,128,128]{1,2,0:T(8,128)S(1)} custom-call(f32[1,128,128]{2,1,0:T(8,128)S(1)} %fusion.44), custom_call_target="InvertDiagBlocksLowerTriangular" | custom-call | tf_op jit(solution)/shard_map/triangular_solve/custom-call.0 | solution.py:45
  107.7 11.9 %cholesky.167 = f32[128,128]{1,0:T(8,128)S(1)} custom-call(f32[128,128]{1,0:T(8,128)S(1)} %fusion.63), custom_call_target="Cholesky" | custom-call | tf_op jit(solution)/shard_map/jit(cholesky)/cholesky | solution.py:44
  121.0 9.8 %custom-call.17 = f32[1,128,128]{1,2,0:T(8,128)S(1)} custom-call(f32[1,128,128]{2,1,0:T(8,128)S(1)} %fusion.45), custom_call_target="InvertDiagBlocksLowerTriangular" | custom-call | tf_op jit(solution)/shard_map/triangular_solve/custom-call.0 | solution.py:45
  133.4 5.9 %fusion.3 = f32[512,2048]{1,0:T(8,128)S(1)} fusion(f32[2048,512]{1,0:T(8,128)} %bitcast.242, f32[256,256]{1,0:T(8,128)S(1)} %select_maximum_fusion.9, f32[128,128]{1,0:T(8,128)S(1)} %copy.131, f32[128,128]{1,0:T(8,128)S(1)} %convolution_negate_fusion.4, f32[128,256]{1,0:T(8,128)S(1)} %concatenate.86, f32[256,256]{1,0:T(8,128)S(1)} %convolution_negate_fusion.1), kind=kOutput, calls=%fused_computation.29 | convolution fusion | flops 3222798336 | bytes 9175040 | tf_op jit(solution)/shard_map/dot_general | solution.py:123
  143.5 15.2 %fusion = f32[256,8,8,128]{3,1,2,0:T(8,128)S(1)} fusion(f32[256,8,8,128]{3,2,1,0:T(8,128)S(1)} %bitcast.246, f32[512,2048]{1,0:T(8,128)S(1)} %fusion.3, f32[1024,512]{1,0:T(8,128)S(1)} %fusion.2), kind=kOutput, calls=%fused_computation.4 | convolution fusion | flops 6444548096 | bytes 23068672 | tf_op jit(solution)/shard_map/dot_general | solution.py:129
  160.8 4.7 copy.137
  165.5 16.2 %gather_fusion = f32[256,128,128]{2,1,0:T(8,128)} fusion(f32[16,128,8,128]{3,1,2,0:T(8,128)} %copy.137, s32[256]{0:T(256)S(1)} %reshape.466), kind=kCustom, calls=%fused_computation | custom fusion | bytes 33556480 | tf_op jit(solution)/shard_map/gather | solution.py:166
  184.0 18.0 %all-gather.6.cloned.1.call-done = f32[24,1,1,1,128,512]{5,4,3,2,1,0:T(8,128)} async-done(((f32[24,1,1,1,8,512]{5,4,3,2,1,0:T(8,128)}), f32[24,1,1,1,128,512]{5,4,3,2,1,0:T(8,128)}) %all-gather.6.cloned.1.call-update) | async-done | bytes 6291472 | tf_op jit(solution)/shard_map/all_gather | solution.py:100
  202.0 9.6 %all-to-all-start = ((f32[128,2,128,128]{3,2,1,0:T(8,128)}), f32[128,2,128,128]{3,2,1,0:T(8,128)}, u32[]{:S(2)}, u32[]{:S(2)}) async-start(f32[128,2,128,128]{3,2,1,0:T(8,128)} %bitcast.238), calls=%async_computation | async-start | bytes 33554432 | tf_op jit(solution)/shard_map/all_to_all | solution.py:180
  215.1 11.7 %cholesky.178 = f32[128,128]{1,0:T(8,128)S(1)} custom-call(f32[128,128]{1,0:T(8,128)S(1)} %fusion.61), custom_call_target="Cholesky" | custom-call | tf_op jit(solution)/shard_map/jit(cholesky)/cholesky | solution.py:44
  228.1 9.8 %custom-call.18 = f32[1,128,128]{1,2,0:T(8,128)S(1)} custom-call(f32[1,128,128]{2,1,0:T(8,128)S(1)} %get-tuple-element.37), custom_call_target="InvertDiagBlocksLowerTriangular" | custom-call | tf_op jit(solution)/shard_map/triangular_solve/custom-call.0 | solution.py:45
  241.9 11.9 %cholesky.189 = f32[128,128]{1,0:T(8,128)S(1)} custom-call(f32[128,128]{1,0:T(8,128)S(1)} %fusion.59), custom_call_target="Cholesky" | custom-call | tf_op jit(solution)/shard_map/jit(cholesky)/cholesky | solution.py:44
  255.1 9.8 %custom-call.19 = f32[1,128,128]{1,2,0:T(8,128)S(1)} custom-call(f32[1,128,128]{2,1,0:T(8,128)S(1)} %get-tuple-element.35), custom_call_target="InvertDiagBlocksLowerTriangular" | custom-call | tf_op jit(solution)/shard_map/triangular_solve/custom-call.0 | solution.py:45
  268.1 11.7 %cholesky.200 = f32[128,128]{1,0:T(8,128)S(1)} custom-call(f32[128,128]{1,0:T(8,128)S(1)} %fusion.57), custom_call_target="Cholesky" | custom-call | tf_op jit(solution)/shard_map/jit(cholesky)/cholesky | solution.py:44
  281.8 9.8 %custom-call.20 = f32[1,128,128]{1,2,0:T(8,128)S(1)} custom-call(f32[1,128,128]{2,1,0:T(8,128)S(1)} %get-tuple-element.33), custom_call_target="InvertDiagBlocksLowerTriangular" | custom-call | tf_op jit(solution)/shard_map/triangular_solve/custom-call.0 | solution.py:45
  292.6 11.9 %cholesky.211 = f32[128,128]{1,0:T(8,128)S(1)} custom-call(f32[128,128]{1,0:T(8,128)S(1)} %fusion.55), custom_call_target="Cholesky" | custom-call | tf_op jit(solution)/shard_map/jit(cholesky)/cholesky | solution.py:44
  306.4 9.8 %custom-call.21 = f32[1,128,128]{1,2,0:T(8,128)S(1)} custom-call(f32[1,128,128]{2,1,0:T(8,128)S(1)} %get-tuple-element.31), custom_call_target="InvertDiagBlocksLowerTriangular" | custom-call | tf_op jit(solution)/shard_map/triangular_solve/custom-call.0 | solution.py:45
  323.5 11.5 %fusion.106 = f32[3072,512]{1,0:T(8,128)S(1)} fusion(f32[3072,512]{1,0:T(8,128)S(1)} %bitcast.249, f32[256,256]{1,0:T(8,128)S(1)} %select_maximum_fusion.7, f32[128,128]{1,0:T(8,128)S(1)} %copy.153, f32[128,128]{1,0:T(8,128)S(1)} %convolution_negate_fusion.2, f32[128,256]{1,0:T(8,128)S(1)} %concatenate.99, f32[256,256]{1,0:T(8,128)S(1)} %convolution_negate_fusion), kind=kOutput, calls=%fused_computation.239 | convolution fusion | flops 9665249280 | bytes 13369344 | tf_op jit(solution)/shard_map/dot_general | solution.py:173
  335.0 12.1 %fusion.118 = f32[3072,512]{1,0:T(8,128)} fusion(f32[3072,512]{1,0:T(8,128)S(1)} %fusion.106, f32[512,512]{1,0:T(8,128)S(1)} %fusion.105), kind=kOutput, calls=%fused_computation.246 | convolution fusion | flops 9663676416 | bytes 13631488 | tf_op jit(solution)/shard_map/dot_general | solution.py:179
  347.1 7.8 %reshape.446 = f32[24,128,4,128]{3,2,1,0:T(4,128)} reshape(f32[3072,512]{1,0:T(8,128)} %fusion.118) | data formatting | bytes 12582912 | tf_op jit(solution)/shard_map/reshape | solution.py:206
  357.7 130.7 %all-to-all-done = f32[128,2,128,128]{3,2,1,0:T(8,128)} async-done(((f32[128,2,128,128]{3,2,1,0:T(8,128)}), f32[128,2,128,128]{3,2,1,0:T(8,128)}, u32[]{:S(2)}, u32[]{:S(2)}) %all-to-all-start) | async-done | bytes 16777248 | tf_op jit(solution)/shard_map/all_to_all | solution.py:180
  488.4 9.4 %gather_fusion.2 = f32[96,128,128]{2,1,0:T(8,128)} fusion(f32[256,128,128]{2,1,0:T(8,128)} %bitcast.28, s32[1024]{0:T(1024)S(1)} %pad_clamp_fusion), kind=kCustom, calls=%fused_computation.2 | custom fusion | bytes 12583296 | tf_op jit(solution)/shard_map/jit(_take)/gather | solution.py:202
  497.8 9.4 %gather_fusion.1 = f32[96,128,128]{2,1,0:T(8,128)} fusion(f32[256,128,128]{2,1,0:T(8,128)} %bitcast.28, s32[1024]{0:T(1024)S(1)} %pad_clamp_fusion.1), kind=kCustom, calls=%fused_computation.1 | custom fusion | bytes 12583296 | tf_op jit(solution)/shard_map/jit(_take)/gather | solution.py:201
  507.2 7.4 %fusion.1 = f32[24,1,128,4,1,1,128]{6,2,3,0,5,4,1:T(8,128)S(1)} fusion(f32[24,128,4,128]{3,2,1,0:T(4,128)} %reshape.446, f32[24,4,128,128]{3,2,1,0:T(8,128)} %bitcast.240, f32[24,4,128,128]{3,2,1,0:T(8,128)} %bitcast.241, pred[24,4]{1,0:T(8,128)(4,1)S(1)} %copy.139, pred[24,4]{1,0:T(8,128)(4,1)S(1)} %copy.119), kind=kLoop, calls=%fused_computation.6 | loop fusion | flops 6291456 | bytes 25166016 | tf_op jit(solution)/shard_map/reshape | solution.py:210
  514.6 7.5 %copy.156 = f32[24,1,128,4,1,1,128]{6,5,4,3,2,1,0:T(1,128)} copy(f32[24,1,128,4,1,1,128]{6,2,3,0,5,4,1:T(8,128)S(1)} %fusion.1) | data formatting | bytes 12582912
  (201 shorter events, 63.2 us)
Async XLA Ops:
  7.2 27.4 %copy-start.6 = (f32[1,512,512]{2,1,0:T(8,128)S(1)}, f32[1,512,512]{2,1,0:T(8,128)}, u32[]{:S(2)}) copy-start(f32[1,512,512]{2,1,0:T(8,128)} %param.9) | copy-start | bytes 3145732
  7.2 174.5 %all-gather.4.cloned.1.call-start = ((), (), s32[]{:S(2)}) async-start(), calls=%async_computation.1 | async-start | bytes 2228224 | tf_op jit(solution)/shard_map/all_gather | solution.py:112
  8.2 12.5 %collective-permute-start.1 = (f32[8,8,512]{2,1,0:T(8,128)S(1)}, f32[8,8,512]{2,1,0:T(8,128)S(1)}, u32[]{:S(2)}, u32[]{:S(2)}) collective-permute-start(f32[8,8,512]{2,1,0:T(8,128)S(1)} %slice_bitcast_fusion.1), channel_id=1, source_target_pairs={{1,8},{2,16},{3,24},{4,32},{5,40},{6,48},{7,56},{8,1},{10,17},{11,... | collective-permute-start | bytes 393224 | tf_op jit(solution)/shard_map/ppermute | solution.py:110
  22.3 179.6 %all-gather.6.cloned.1.call-start = ((), (), s32[]{:S(2)}) async-start(), calls=%async_computation.2 | async-start | bytes 6684672 | tf_op jit(solution)/shard_map/all_gather | solution.py:100
  26.2 113.2 %collective-permute-start = (f32[8,128,512]{2,1,0:T(8,128)}, f32[8,128,512]{2,1,0:T(8,128)}, u32[]{:S(2)}, u32[]{:S(2)}) collective-permute-start(f32[8,128,512]{2,1,0:T(8,128)} %slice_bitcast_fusion), channel_id=1, source_target_pairs={{1,8},{2,16},{3,24},{4,32},{5,40},{6,48},{7,56},{8,1},{10,17},{11,... | collective-permute-start | bytes 6291464 | tf_op jit(solution)/shard_map/ppermute | solution.py:96
  131.3 8.1 %copy-start = (f32[1,16,1,128,512]{4,3,2,1,0:T(8,128)S(1)}, f32[1,16,1,128,512]{4,3,2,1,0:T(8,128)}, u32[]{:S(2)}) copy-start(f32[1,16,1,128,512]{4,3,2,1,0:T(8,128)} %param.10) | copy-start | bytes 12582916
  133.4 10.1 %slice-start = ((s8[8388608]{0:T(1024)(128)(4,1)}), s8[4194304]{0:T(1024)(128)(4,1)S(1)}, s32[]{:S(2)}) async-start(s8[8388608]{0:T(1024)(128)(4,1)} %bitcast.244), calls=%async_computation.3 | async-start | bytes 8388608
  139.3 4.1 slice-start.1
  202.0 9.6 %copy-start.9 = (s32[2,128]{1,0:T(2,128)S(1)}, s32[2,128]{1,0:T(2,128)}, u32[]{:S(2)}) copy-start(s32[2,128]{1,0:T(2,128)} %param.14) | copy-start | bytes 3076
  202.0 12.6 %copy-start.2 = (f32[512,512]{1,0:T(8,128)S(1)}, f32[512,512]{1,0:T(8,128)}, u32[]{:S(2)}) copy-start(f32[512,512]{1,0:T(8,128)} %param.12) | copy-start | bytes 3145732
  202.0 286.4 %all-to-all-start = ((f32[128,2,128,128]{3,2,1,0:T(8,128)}), f32[128,2,128,128]{3,2,1,0:T(8,128)}, u32[]{:S(2)}, u32[]{:S(2)}) async-start(f32[128,2,128,128]{3,2,1,0:T(8,128)} %bitcast.238), calls=%async_computation | async-start | bytes 33554432 | tf_op jit(solution)/shard_map/all_to_all | solution.py:180
  215.0 108.5 %slice-start.2 = ((s8[6291456]{0:T(1024)(128)(4,1)}), s8[2097152]{0:T(1024)(128)(4,1)S(1)}, s32[]{:S(2)}) async-start(s8[6291456]{0:T(1024)(128)(4,1)} %bitcast.247), calls=%async_computation.5 | async-start | bytes 4194304
  240.2 0.8 copy-start.1
  316.6 6.9 %slice-start.3 = ((s8[6291456]{0:T(1024)(128)(4,1)}), s8[4194304]{0:T(1024)(128)(4,1)S(1)}, s32[]{:S(2)}) async-start(s8[6291456]{0:T(1024)(128)(4,1)} %bitcast.247), calls=%async_computation.6 | async-start | bytes 8388608
  317.2 17.8 %copy-start.4 = (f32[256,256]{1,0:T(8,128)}, f32[256,256]{1,0:T(8,128)S(1)}, u32[]{:S(2)}) copy-start(f32[256,256]{1,0:T(8,128)S(1)} %select_maximum_fusion.7) | copy-start | bytes 786436
  347.1 7.8 %copy-start.7 = (f32[512,128]{1,0:T(8,128)S(1)}, f32[512,128]{1,0:T(8,128)}, u32[]{:S(2)}) copy-start(f32[512,128]{1,0:T(8,128)} %get-tuple-element.55) | copy-start | bytes 786436
  347.1 7.8 %copy-start.8 = (f32[128,128]{1,0:T(8,128)S(1)}, f32[128,128]{1,0:T(8,128)}, u32[]{:S(2)}) copy-start(f32[128,128]{1,0:T(8,128)} %get-tuple-element.32) | copy-start | bytes 196612
  347.1 8.9 %copy-start.3 = (f32[24,1,1,1,8,512]{5,4,3,2,1,0:T(8,128)S(1)}, f32[24,1,1,1,8,512]{5,4,3,2,1,0:T(8,128)}, u32[]{:S(2)}) copy-start(f32[24,1,1,1,8,512]{5,4,3,2,1,0:T(8,128)} %param.13) | copy-start | bytes 1179652
  347.1 8.9 %copy-start.5 = (f32[256,256]{1,0:T(8,128)S(1)}, f32[256,256]{1,0:T(8,128)}, u32[]{:S(2)}) copy-start(f32[256,256]{1,0:T(8,128)} %copy-done.4) | copy-start | bytes 786436
Sparse Core Ops, SparseCore 0:
  22.4 136.6 all-gather.3
  160.9 41.0 all-gather.5
where the time goes:
time: 539 us; the launch traced here: 529 us
  other arithmetic  202 us (37%)
  waiting for transfers between devices  157 us (29%)
  local copies, waits for them, and re-layouts  70.5 us (13%)
  matrix products  64.7 us (12%)
  starting transfers between devices  19 us (4%)
  between operations  15.3 us (3%)
    all_to_all x1, waiting for transfers between devices, per_device(): lax.all_to_all(outgoing.reshape(-1, per_row * per_col, BLOCK_EXTENT, BLOC...  131 us
    another operation x24, other arithmetic, factor_and_inverse(): low = jnp.linalg.cholesky(work[:leaf, :leaf])  99.7 us
    another operation x16, other arithmetic, factor_and_inverse(): inv = lax.linalg.triangular_solve(low, eye, left_side=True, lower=True)  85.1 us
    all_gather x1, waiting for transfers between devices, per_device(): lax.all_gather(parent_lead_panel.reshape(parent_row_blocks, sub_rows, pan...  18 us
    gather x1, local copies, waits for them, and re-layouts, per_device(): outgoing = schur_blocks[send_row_index, :, send_col_index, :]  16.2 us
    dot_general x1, matrix products, per_device(): lax.dot_general(child_factor, child_columns, dims, precision=high)  15.2 us
    dot_general x1, matrix products, per_device(): update = lax.dot_general(row_factor, column_factor, dims, precision=highest)  12.1 us
    dot_general x1, matrix products, per_device(): lax.dot_general(gathered.reshape(-1, panel_width), parent_inv, dims, prec...  11.5 us
  transfers between devices with their start and end apart: 5, of which 3 were waited for; matrix products, arithmetic and copies ran while one was open for 57% of the time, Pallas kernels for 0%

commit v1 on v0

--- a/solution.py
+++ b/solution.py
@@ -8,6 +8,13 @@
 SB = 128
 RB = 192
 WB = 64
+
+
+def gather_over(x, name, dim):
+    size = lax.axis_size(name)
+    shards = jnp.stack([x for _ in range(size)])
+    shards = lax.all_to_all(shards, name, split_axis=0, concat_axis=0)
+    return jnp.concatenate(shards, axis=dim)
 
 
 def from_root(shard, axis, root):
@@ -97,11 +104,8 @@
     )
     sub_rows = parent_lead_panel.shape[4]
     own_rows = parent_lead_panel.reshape(-1, panel_width)
-    gathered = lax.all_gather(
-        parent_lead_panel.reshape(parent_row_blocks, sub_rows, panel_width),
-        ("half", "col"),
-        axis=1,
-        tiled=True,
+    gathered = gather_over(
+        parent_lead_panel.reshape(parent_row_blocks, sub_rows, panel_width), ("half", "col"), 1
     )
     leading_parent = parent_lead_panel.reshape(parent_row_blocks, sub_rows, panel_width)[
         : 2 * parent_cols

time: 539 us -> 553 us (1.026)
  starting transfers between devices: 19 us -> 40.6 us
  waiting for transfers between devices: 157 us -> 139 us
  local copies, waits for them, and re-layouts: 70.5 us -> 80.6 us
    all_gather x1 -> x0, waiting for transfers between devices: 18 us -> none  [per_device(): lax.all_gather(parent_lead_panel.reshape(parent_row_blocks, sub_rows, pan...]
    all_to_all x1, starting transfers between devices: 9.58 us -> 22.5 us  [per_device(): lax.all_to_all(outgoing.reshape(-1, per_row * per_col, BLOCK_EXTENT, BLOC...]
    all_to_all x0 -> x1, starting transfers between devices: none -> 10.5 us  [gather_over(): shards = lax.all_to_all(shards, name, split_axis=0, concat_axis=0)]
    all_gather x1, waiting for transfers between devices: 0.01 us -> 8.35 us  [per_device(): lax.all_gather(transposed, ('half', 'row'), axis=1, tiled=True)]
    ppermute x1, waiting for transfers between devices: 7.85 us -> 0.01 us  [per_device(): lax.ppermute(leading_parent, ('row', 'col'), transpose_perm)]
    all_to_all x0 -> x1, local copies, waits for them, and re-layouts: none -> 6.53 us  [gather_over(): shards = lax.all_to_all(shards, name, split_axis=0, concat_axis=0)]
  transfers between devices with their start and end apart: 5 -> 5, of which waited for: 3 -> 2; matrix products, arithmetic and copies ran while one was open for 57% -> 56% of each run, Pallas kernels for 0% -> 0%
where the time goes in v1:
time: 553 us; the launch traced here: 543 us
  other arithmetic  202 us (37%)
  waiting for transfers between devices  139 us (25%)
  local copies, waits for them, and re-layouts  80.6 us (15%)
  matrix products  64.7 us (12%)
  starting transfers between devices  40.6 us (7%)
  between operations  15.3 us (3%)
    all_to_all x1, waiting for transfers between devices, per_device(): lax.all_to_all(outgoing.reshape(-1, per_row * per_col, BLOCK_EXTENT, BLOC...  131 us
    another operation x24, other arithmetic, factor_and_inverse(): low = jnp.linalg.cholesky(work[:leaf, :leaf])  99.6 us
    another operation x16, other arithmetic, factor_and_inverse(): inv = lax.linalg.triangular_solve(low, eye, left_side=True, lower=True)  85.1 us
    all_to_all x1, starting transfers between devices, per_device(): lax.all_to_all(outgoing.reshape(-1, per_row * per_col, BLOCK_EXTENT, BLOC...  22.5 us
    gather x1, local copies, waits for them, and re-layouts, per_device(): outgoing = schur_blocks[send_row_index, :, send_col_index, :]  16 us
    dot_general x1, matrix products, per_device(): lax.dot_general(child_factor, child_columns, dims, precision=high)  15.2 us
    dot_general x1, matrix products, per_device(): update = lax.dot_general(row_factor, column_factor, dims, precision=highest)  12.1 us
    dot_general x1, matrix products, per_device(): lax.dot_general(gathered.reshape(-1, panel_width), parent_inv, dims, prec...  11.5 us
  transfers between devices with their start and end apart: 5, of which 2 were waited for; matrix products, arithmetic and copies ran while one was open for 56% of the time, Pallas kernels for 0%

profile of v1, /device:TPU:10, one launch (start us, length us, event | category | flops | bytes accessed | tf_op | source)
XLA Modules:
  0.0 542.6 jit_solution(6667339026826774119)
XLA Ops:
  23.4 10.5 %all-to-all-start = ((f32[16,24,8,512]{3,2,1,0:T(8,128)}), f32[16,24,8,512]{3,2,1,0:T(8,128)}, u32[]{:S(2)}, u32[]{:S(2)}) async-start(f32[16,24,8,512]{3,2,1,0:T(8,128)} %stack.3), calls=%async_computation | async-start | bytes 12582912 | tf_op jit(solution)/shard_map/all_to_all | solution.py:16
  36.3 11.7 %cholesky.134 = f32[128,128]{1,0:T(8,128)S(1)} custom-call(f32[128,128]{1,0:T(8,128)S(1)} %fusion.69), custom_call_target="Cholesky" | custom-call | tf_op jit(solution)/shard_map/jit(cholesky)/cholesky | solution.py:51
  49.4 9.8 %custom-call.14 = f32[1,128,128]{1,2,0:T(8,128)S(1)} custom-call(f32[1,128,128]{2,1,0:T(8,128)S(1)} %get-tuple-element.45), custom_call_target="InvertDiagBlocksLowerTriangular" | custom-call | tf_op jit(solution)/shard_map/triangular_solve/custom-call.0 | solution.py:52
  60.6 11.7 %cholesky.145 = f32[128,128]{1,0:T(8,128)S(1)} custom-call(f32[128,128]{1,0:T(8,128)S(1)} %fusion.67), custom_call_target="Cholesky" | custom-call | tf_op jit(solution)/shard_map/jit(cholesky)/cholesky | solution.py:51
  73.7 9.9 %custom-call.15 = f32[1,128,128]{1,2,0:T(8,128)S(1)} custom-call(f32[1,128,128]{2,1,0:T(8,128)S(1)} %get-tuple-element.43), custom_call_target="InvertDiagBlocksLowerTriangular" | custom-call | tf_op jit(solution)/shard_map/triangular_solve/custom-call.0 | solution.py:52
  84.8 11.7 %cholesky.156 = f32[128,128]{1,0:T(8,128)S(1)} custom-call(f32[128,128]{1,0:T(8,128)S(1)} %fusion.65), custom_call_target="Cholesky" | custom-call | tf_op jit(solution)/shard_map/jit(cholesky)/cholesky | solution.py:51
  97.9 9.8 %custom-call.16 = f32[1,128,128]{1,2,0:T(8,128)S(1)} custom-call(f32[1,128,128]{2,1,0:T(8,128)S(1)} %fusion.44), custom_call_target="InvertDiagBlocksLowerTriangular" | custom-call | tf_op jit(solution)/shard_map/triangular_solve/custom-call.0 | solution.py:52
  108.9 11.9 %cholesky.167 = f32[128,128]{1,0:T(8,128)S(1)} custom-call(f32[128,128]{1,0:T(8,128)S(1)} %fusion.63), custom_call_target="Cholesky" | custom-call | tf_op jit(solution)/shard_map/jit(cholesky)/cholesky | solution.py:51
  124.9 9.8 %custom-call.17 = f32[1,128,128]{1,2,0:T(8,128)S(1)} custom-call(f32[1,128,128]{2,1,0:T(8,128)S(1)} %fusion.45), custom_call_target="InvertDiagBlocksLowerTriangular" | custom-call | tf_op jit(solution)/shard_map/triangular_solve/custom-call.0 | solution.py:52
  137.3 5.9 %fusion.3 = f32[512,2048]{1,0:T(8,128)S(1)} fusion(f32[2048,512]{1,0:T(8,128)} %bitcast.250, f32[256,256]{1,0:T(8,128)S(1)} %select_maximum_fusion.9, f32[128,128]{1,0:T(8,128)S(1)} %copy.132, f32[128,128]{1,0:T(8,128)S(1)} %convolution_negate_fusion.4, f32[128,256]{1,0:T(8,128)S(1)} %concatenate.86, f32[256,256]{1,0:T(8,128)S(1)} %convolution_negate_fusion.1), kind=kOutput, calls=%fused_computation.30 | convolution fusion | flops 3222798336 | bytes 9175040 | tf_op jit(solution)/shard_map/dot_general | solution.py:127
  147.4 15.2 %fusion = f32[256,8,8,128]{3,1,2,0:T(8,128)S(1)} fusion(f32[256,8,8,128]{3,2,1,0:T(8,128)S(1)} %bitcast.254, f32[512,2048]{1,0:T(8,128)S(1)} %fusion.3, f32[1024,512]{1,0:T(8,128)S(1)} %fusion.2), kind=kOutput, calls=%fused_computation.4 | convolution fusion | flops 6444548096 | bytes 23068672 | tf_op jit(solution)/shard_map/dot_general | solution.py:133
  164.6 4.7 copy.138
  169.3 16.0 %gather_fusion = f32[256,128,128]{2,1,0:T(8,128)} fusion(f32[16,128,8,128]{3,1,2,0:T(8,128)} %copy.138, s32[256]{0:T(256)S(1)} %reshape.472), kind=kCustom, calls=%fused_computation | custom fusion | bytes 33556480 | tf_op jit(solution)/shard_map/gather | solution.py:170
  185.4 8.3 %all-gather.2.cloned.1.call-done = f32[8,128,512]{2,1,0:T(8,128)} async-done(((f32[8,8,512]{2,1,0:T(8,128)}), f32[8,128,512]{2,1,0:T(8,128)}) %all-gather.2.cloned.1.call-update) | async-done | bytes 2097168 | tf_op jit(solution)/shard_map/all_gather | solution.py:116
  196.0 6.5 %copy.177 = f32[16,24,8,512]{3,2,0,1:T(8,128)} copy(f32[16,24,8,512]{3,2,1,0:T(8,128)} %all-to-all-done) | data formatting | bytes 12582912 | tf_op jit(solution)/shard_map/all_to_all | solution.py:16
  202.5 22.5 %all-to-all-start.1 = ((f32[128,2,128,128]{3,2,1,0:T(8,128)}), f32[128,2,128,128]{3,2,1,0:T(8,128)}, u32[]{:S(2)}, u32[]{:S(2)}) async-start(f32[128,2,128,128]{3,2,1,0:T(8,128)} %bitcast.243), calls=%async_computation.1 | async-start | bytes 33554432 | tf_op jit(solution)/shard_map/all_to_all | solution.py:184
  228.5 11.7 %cholesky.178 = f32[128,128]{1,0:T(8,128)S(1)} custom-call(f32[128,128]{1,0:T(8,128)S(1)} %fusion.61), custom_call_target="Cholesky" | custom-call | tf_op jit(solution)/shard_map/jit(cholesky)/cholesky | solution.py:51
  241.6 9.8 %custom-call.18 = f32[1,128,128]{1,2,0:T(8,128)S(1)} custom-call(f32[1,128,128]{2,1,0:T(8,128)S(1)} %get-tuple-element.37), custom_call_target="InvertDiagBlocksLowerTriangular" | custom-call | tf_op jit(solution)/shard_map/triangular_solve/custom-call.0 | solution.py:52
  255.4 11.9 %cholesky.189 = f32[128,128]{1,0:T(8,128)S(1)} custom-call(f32[128,128]{1,0:T(8,128)S(1)} %fusion.59), custom_call_target="Cholesky" | custom-call | tf_op jit(solution)/shard_map/jit(cholesky)/cholesky | solution.py:51
  268.6 9.8 %custom-call.19 = f32[1,128,128]{1,2,0:T(8,128)S(1)} custom-call(f32[1,128,128]{2,1,0:T(8,128)S(1)} %get-tuple-element.35), custom_call_target="InvertDiagBlocksLowerTriangular" | custom-call | tf_op jit(solution)/shard_map/triangular_solve/custom-call.0 | solution.py:52
  281.5 11.7 %cholesky.200 = f32[128,128]{1,0:T(8,128)S(1)} custom-call(f32[128,128]{1,0:T(8,128)S(1)} %fusion.57), custom_call_target="Cholesky" | custom-call | tf_op jit(solution)/shard_map/jit(cholesky)/cholesky | solution.py:51
  295.2 9.8 %custom-call.20 = f32[1,128,128]{1,2,0:T(8,128)S(1)} custom-call(f32[1,128,128]{2,1,0:T(8,128)S(1)} %get-tuple-element.33), custom_call_target="InvertDiagBlocksLowerTriangular" | custom-call | tf_op jit(solution)/shard_map/triangular_solve/custom-call.0 | solution.py:52
  306.0 11.9 %cholesky.211 = f32[128,128]{1,0:T(8,128)S(1)} custom-call(f32[128,128]{1,0:T(8,128)S(1)} %fusion.55), custom_call_target="Cholesky" | custom-call | tf_op jit(solution)/shard_map/jit(cholesky)/cholesky | solution.py:51
  319.9 9.8 %custom-call.21 = f32[1,128,128]{1,2,0:T(8,128)S(1)} custom-call(f32[1,128,128]{2,1,0:T(8,128)S(1)} %get-tuple-element.31), custom_call_target="InvertDiagBlocksLowerTriangular" | custom-call | tf_op jit(solution)/shard_map/triangular_solve/custom-call.0 | solution.py:52
  336.9 11.5 %fusion.106 = f32[3072,512]{1,0:T(8,128)S(1)} fusion(f32[3072,512]{1,0:T(8,128)S(1)} %bitcast.247, f32[256,256]{1,0:T(8,128)S(1)} %select_maximum_fusion.7, f32[128,128]{1,0:T(8,128)S(1)} %copy.155, f32[128,128]{1,0:T(8,128)S(1)} %convolution_negate_fusion.2, f32[128,256]{1,0:T(8,128)S(1)} %concatenate.99, f32[256,256]{1,0:T(8,128)S(1)} %convolution_negate_fusion), kind=kOutput, calls=%fused_computation.240 | convolution fusion | flops 9665249280 | bytes 13369344 | tf_op jit(solution)/shard_map/dot_general | solution.py:177
  348.4 12.1 %fusion.118 = f32[3072,512]{1,0:T(8,128)} fusion(f32[3072,512]{1,0:T(8,128)S(1)} %fusion.106, f32[512,512]{1,0:T(8,128)S(1)} %fusion.105), kind=kOutput, calls=%fused_computation.247 | convolution fusion | flops 9663676416 | bytes 13631488 | tf_op jit(solution)/shard_map/dot_general | solution.py:183
  360.5 7.8 %reshape.452 = f32[24,128,4,128]{3,2,1,0:T(4,128)} reshape(f32[3072,512]{1,0:T(8,128)} %fusion.118) | data formatting | bytes 12582912 | tf_op jit(solution)/shard_map/reshape | solution.py:210
  371.1 130.7 %all-to-all-done.1 = f32[128,2,128,128]{3,2,1,0:T(8,128)} async-done(((f32[128,2,128,128]{3,2,1,0:T(8,128)}), f32[128,2,128,128]{3,2,1,0:T(8,128)}, u32[]{:S(2)}, u32[]{:S(2)}) %all-to-all-start.1) | async-done | bytes 16777248 | tf_op jit(solution)/shard_map/all_to_all | solution.py:184
  501.9 9.4 %gather_fusion.2 = f32[96,128,128]{2,1,0:T(8,128)} fusion(f32[256,128,128]{2,1,0:T(8,128)} %bitcast.30, s32[1024]{0:T(1024)S(1)} %pad_clamp_fusion), kind=kCustom, calls=%fused_computation.2 | custom fusion | bytes 12583296 | tf_op jit(solution)/shard_map/jit(_take)/gather | solution.py:206
  511.3 9.4 %gather_fusion.1 = f32[96,128,128]{2,1,0:T(8,128)} fusion(f32[256,128,128]{2,1,0:T(8,128)} %bitcast.30, s32[1024]{0:T(1024)S(1)} %pad_clamp_fusion.1), kind=kCustom, calls=%fused_computation.1 | custom fusion | bytes 12583296 | tf_op jit(solution)/shard_map/jit(_take)/gather | solution.py:205
  520.7 7.4 %fusion.1 = f32[24,1,128,4,1,1,128]{6,2,3,0,5,4,1:T(8,128)S(1)} fusion(f32[24,128,4,128]{3,2,1,0:T(4,128)} %reshape.452, f32[24,4,128,128]{3,2,1,0:T(8,128)} %bitcast.248, f32[24,4,128,128]{3,2,1,0:T(8,128)} %bitcast.249, pred[24,4]{1,0:T(8,128)(4,1)S(1)} %copy.141, pred[24,4]{1,0:T(8,128)(4,1)S(1)} %copy.120), kind=kLoop, calls=%fused_computation.6 | loop fusion | flops 6291456 | bytes 25166016 | tf_op jit(solution)/shard_map/reshape | solution.py:214
  528.0 7.5 %copy.158 = f32[24,1,128,4,1,1,128]{6,5,4,3,2,1,0:T(1,128)} copy(f32[24,1,128,4,1,1,128]{6,2,3,0,5,4,1:T(8,128)S(1)} %fusion.1) | data formatting | bytes 12582912
  (202 shorter events, 69.2 us)
Async XLA Ops:
  8.1 114.5 %collective-permute-start.1 = (f32[8,8,512]{2,1,0:T(8,128)S(1)}, f32[8,8,512]{2,1,0:T(8,128)S(1)}, u32[]{:S(2)}, u32[]{:S(2)}) collective-permute-start(f32[8,8,512]{2,1,0:T(8,128)S(1)} %slice_bitcast_fusion.1), channel_id=1, source_target_pairs={{1,8},{2,16},{3,24},{4,32},{5,40},{6,48},{7,56},{8,1},{10,17},{11,... | collective-permute-start | bytes 393224 | tf_op jit(solution)/shard_map/ppermute | solution.py:114
  15.8 127.4 %collective-permute-start = (f32[8,128,512]{2,1,0:T(8,128)}, f32[8,128,512]{2,1,0:T(8,128)}, u32[]{:S(2)}, u32[]{:S(2)}) collective-permute-start(f32[8,128,512]{2,1,0:T(8,128)} %slice_bitcast_fusion), channel_id=1, source_target_pairs={{1,8},{2,16},{3,24},{4,32},{5,40},{6,48},{7,56},{8,1},{10,17},{11,... | collective-permute-start | bytes 6291464 | tf_op jit(solution)/shard_map/ppermute | solution.py:103
  23.3 11.0 %copy-start.9 = (s32[2,128]{1,0:T(2,128)S(1)}, s32[2,128]{1,0:T(2,128)}, u32[]{:S(2)}) copy-start(s32[2,128]{1,0:T(2,128)} %param.14) | copy-start | bytes 3076
  23.4 12.5 %copy-start.6 = (f32[1,512,512]{2,1,0:T(8,128)S(1)}, f32[1,512,512]{2,1,0:T(8,128)}, u32[]{:S(2)}) copy-start(f32[1,512,512]{2,1,0:T(8,128)} %param.9) | copy-start | bytes 3145732
  23.4 172.6 %all-to-all-start = ((f32[16,24,8,512]{3,2,1,0:T(8,128)}), f32[16,24,8,512]{3,2,1,0:T(8,128)}, u32[]{:S(2)}, u32[]{:S(2)}) async-start(f32[16,24,8,512]{3,2,1,0:T(8,128)} %stack.3), calls=%async_computation | async-start | bytes 12582912 | tf_op jit(solution)/shard_map/all_to_all | solution.py:16
  33.8 159.9 %all-gather.2.cloned.1.call-start = ((), (), s32[]{:S(2)}) async-start(), calls=%async_computation.2 | async-start | bytes 2228224 | tf_op jit(solution)/shard_map/all_gather | solution.py:116
  135.1 8.1 %copy-start = (f32[1,16,1,128,512]{4,3,2,1,0:T(8,128)S(1)}, f32[1,16,1,128,512]{4,3,2,1,0:T(8,128)}, u32[]{:S(2)}) copy-start(f32[1,16,1,128,512]{4,3,2,1,0:T(8,128)} %param.10) | copy-start | bytes 12582916
  137.3 10.1 %slice-start.2 = ((s8[8388608]{0:T(1024)(128)(4,1)}), s8[4194304]{0:T(1024)(128)(4,1)S(1)}, s32[]{:S(2)}) async-start(s8[8388608]{0:T(1024)(128)(4,1)} %bitcast.252), calls=%async_computation.5 | async-start | bytes 8388608
  143.2 4.1 slice-start.3
  202.5 25.5 %copy-start.2 = (f32[512,512]{1,0:T(8,128)S(1)}, f32[512,512]{1,0:T(8,128)}, u32[]{:S(2)}) copy-start(f32[512,512]{1,0:T(8,128)} %param.12) | copy-start | bytes 3145732
  202.5 299.3 %all-to-all-start.1 = ((f32[128,2,128,128]{3,2,1,0:T(8,128)}), f32[128,2,128,128]{3,2,1,0:T(8,128)}, u32[]{:S(2)}, u32[]{:S(2)}) async-start(f32[128,2,128,128]{3,2,1,0:T(8,128)} %bitcast.243), calls=%async_computation.1 | async-start | bytes 33554432 | tf_op jit(solution)/shard_map/all_to_all | solution.py:184
  228.4 108.5 %slice-start = ((s8[6291456]{0:T(1024)(128)(4,1)}), s8[2097152]{0:T(1024)(128)(4,1)S(1)}, s32[]{:S(2)}) async-start(s8[6291456]{0:T(1024)(128)(4,1)} %bitcast.245), calls=%async_computation.3 | async-start | bytes 4194304
  253.6 0.8 copy-start.1
  330.0 6.9 %slice-start.1 = ((s8[6291456]{0:T(1024)(128)(4,1)}), s8[4194304]{0:T(1024)(128)(4,1)S(1)}, s32[]{:S(2)}) async-start(s8[6291456]{0:T(1024)(128)(4,1)} %bitcast.245), calls=%async_computation.4 | async-start | bytes 8388608
  330.6 17.8 %copy-start.4 = (f32[256,256]{1,0:T(8,128)}, f32[256,256]{1,0:T(8,128)S(1)}, u32[]{:S(2)}) copy-start(f32[256,256]{1,0:T(8,128)S(1)} %select_maximum_fusion.7) | copy-start | bytes 786436
  360.5 7.8 %copy-start.7 = (f32[512,128]{1,0:T(8,128)S(1)}, f32[512,128]{1,0:T(8,128)}, u32[]{:S(2)}) copy-start(f32[512,128]{1,0:T(8,128)} %get-tuple-element.55) | copy-start | bytes 786436
  360.5 7.8 %copy-start.8 = (f32[128,128]{1,0:T(8,128)S(1)}, f32[128,128]{1,0:T(8,128)}, u32[]{:S(2)}) copy-start(f32[128,128]{1,0:T(8,128)} %get-tuple-element.32) | copy-start | bytes 196612
  360.5 8.9 %copy-start.3 = (f32[24,1,1,1,8,512]{5,4,3,2,1,0:T(8,128)S(1)}, f32[24,1,1,1,8,512]{5,4,3,2,1,0:T(8,128)}, u32[]{:S(2)}) copy-start(f32[24,1,1,1,8,512]{5,4,3,2,1,0:T(8,128)} %param.13) | copy-start | bytes 1179652
  360.5 8.9 %copy-start.5 = (f32[256,256]{1,0:T(8,128)S(1)}, f32[256,256]{1,0:T(8,128)}, u32[]{:S(2)}) copy-start(f32[256,256]{1,0:T(8,128)} %copy-done.4) | copy-start | bytes 786436
Sparse Core Ops, SparseCore 0:
  124.3 69.3 all-gather.1
